TPU v7x, 32 devices: a whole 2x2x4 slice. The times are simulated.
32 devices in a mesh: row: 8 (over z, x), col: 4 (over y, core).
Axes of the slice: x: 2, y: 2, z: 4, core: 2. Of those that a mesh axis runs over, the one named last changes fastest.
Arguments:
- low_rhs: bfloat16 [32, 512, 128], P(('row', 'col')), may hold values from -6 to 6
- low_inv: bfloat16 [32, 512, 512], P(('row', 'col'))
- low_tiles: bfloat16 [32, 4, 512, 512], P(('row', 'col')), may hold values from -0.03125 to 0.03125
- tile_rows: int32 [32, 4], P(('row', 'col')), may hold values from -1 to 3, as said below
- tile_cols: int32 [32, 4], P(('row', 'col')), may hold values from 0 to 31, as said below
- top_rhs: bfloat16 [4, 512, 128], P(None, 'row'), may hold values from -6 to 6
- top_inv: bfloat16 [4, 512, 512], P(None, 'row')
- top_tiles: bfloat16 [6, 512, 512], P(None, 'row'), may hold values from -0.125 to 0.125
Outputs:
- low_solution: float32 [32, 512, 128], P(('row', 'col'))
- top_solution: float32 [4, 512, 128], P(None, 'row')
Inputs may be any that keep to these rules, and one draw needn't show every extreme that they name: `tile_rows`: in each block's list of 4 slots the used slots come first and name top-level blocks; the remaining slots hold -1. Some list has only its first slot used and some list is full. Slot s of block j names a block of j's aligned group of 4 blocks (j // 4 == tile_cols[j, s] // 4); an empty slot names j itself.
All inputs are finite; a program needn't handle non-finite values.
Results may differ from a plain program's by a relative error of at most 0.022.
Values may be sent and summed in bfloat16 or wider, within the bound.
No kernel may reach another device: no remote copies, remote signals or barrier semaphores. Data moves between devices by JAX's collectives and lax.ppermute only.
A program may use at most 64 MiB of HBM per device.

v0:
```python
import jax
import jax.numpy as jnp
from jax import lax
from jax.sharding import PartitionSpec as P


def local(low_rhs, low_inv, low_tiles, tile_rows, tile_cols, top_rhs, top_inv, top_tiles):
    peers = lax.axis_size("col")
    levels = top_rhs.shape[0]
    share = top_rhs.shape[1]
    position = lax.axis_index("row")
    slot_rows = tile_rows[0]
    slot_cols = tile_cols[0] % peers
    alive = slot_rows >= 0
    safe_rows = jnp.maximum(slot_rows, 0)
    own_tiles = low_tiles[0]
    low_forward = jnp.dot(low_inv[0], low_rhs[0], preferred_element_type=jnp.float32).astype(
        jnp.bfloat16
    )
    panels = lax.all_gather(low_forward[None], "col", axis=0, tiled=True)
    products = jnp.einsum(
        "sab,sbk->sak", own_tiles, panels[slot_cols], preferred_element_type=jnp.float32
    )
    pick_level = (slot_rows[:, None] == jnp.arange(levels, dtype=jnp.int32)[None, :]).astype(
        jnp.float32
    )
    coupling = jnp.einsum("st,sak->tak", pick_level, products, precision=lax.Precision.HIGHEST)
    whole_sum = lax.psum(coupling.astype(jnp.bfloat16), "col")
    coupled = lax.psum_scatter(whole_sum, "row", scatter_dimension=1, tiled=True).astype(
        jnp.float32
    )
    top_back = [None] * levels
    top_slices = [None] * levels
    top_forward = []
    for level in range(levels):
        residue = top_rhs[level].astype(jnp.float32) - coupled[level]
        if level > 0:
            first = level * (level - 1) // 2
            earlier = jnp.stack(top_forward)
            residue = residue - jnp.einsum(
                "uab,ubk->ak",
                top_tiles[first : first + level],
                earlier,
                preferred_element_type=jnp.float32,
            )
        whole_residue = lax.all_gather(residue.astype(jnp.bfloat16), "row", axis=0, tiled=True)
        solved_part = jnp.dot(
            top_inv[level], whole_residue, preferred_element_type=jnp.float32
        ).astype(jnp.bfloat16)
        top_forward.append(lax.all_gather(solved_part, "row", axis=0, tiled=True))
    for level in reversed(range(levels)):
        update = lax.dynamic_slice_in_dim(top_forward[level], position * share, share, 0).astype(
            jnp.float32
        )
        if level < levels - 1:
            later = list(range(level + 1, levels))
            tiles_below = jnp.stack([top_tiles[k * (k - 1) // 2 + level] for k in later])
            slices_below = jnp.stack(
                [lax.dynamic_slice_in_dim(top_back[k], position * share, share, 0) for k in later]
            )
            partial_term = jnp.einsum(
                "kab,kac->bc", tiles_below, slices_below, preferred_element_type=jnp.float32
            )
            update = update - lax.psum_scatter(
                partial_term.astype(jnp.bfloat16), "row", scatter_dimension=0, tiled=True
            ).astype(jnp.float32)
        local_part = jnp.einsum(
            "ab,ac->bc",
            top_inv[level],
            update.astype(jnp.bfloat16),
            preferred_element_type=jnp.float32,
        )
        solution = lax.psum(local_part.astype(jnp.bfloat16), "row").astype(jnp.float32)
        top_slices[level] = lax.dynamic_slice_in_dim(solution, position * share, share, 0)
        top_back[level] = solution.astype(jnp.bfloat16)
    back_stack = jnp.stack(top_back)
    products_back = jnp.einsum(
        "sab,sak->sbk", own_tiles, back_stack[safe_rows], preferred_element_type=jnp.float32
    )
    pick_peer = (
        (slot_cols[:, None] == jnp.arange(peers, dtype=jnp.int32)[None, :]) & alive[:, None]
    ).astype(jnp.float32)
    terms = jnp.einsum("sp,sbk->pbk", pick_peer, products_back, precision=lax.Precision.HIGHEST)
    returned = lax.psum_scatter(
        terms.astype(jnp.bfloat16), "col", scatter_dimension=0, tiled=True
    ).astype(jnp.float32)
    low_update = (low_forward.astype(jnp.float32) - returned[0]).astype(jnp.bfloat16)
    low_solution = jnp.einsum(
        "ab,ac->bc", low_inv[0], low_update, preferred_element_type=jnp.float32
    )
    return (low_solution[None], jnp.stack(top_slices))


def solution(mesh):
    in_specs = (
        P(("row", "col"), None, None),
        P(("row", "col"), None, None),
        P(("row", "col"), None, None, None),
        P(("row", "col"), None),
        P(("row", "col"), None),
        P(None, "row", None),
        P(None, "row", None),
        P(None, "row", None),
    )
    out_specs = (P(("row", "col"), None, None), P(None, "row", None))
    return jax.shard_map(local, mesh=mesh, in_specs=in_specs, out_specs=out_specs, check_vma=False)
```

profile of v0, /device:TPU:0, one launch (start us, length us, event | category | flops | bytes accessed | tf_op | source)
XLA Modules:
  0.0 905.1 jit_solution(3152110872918101658)
XLA Ops:
  7.2 1.5 convolution_convert_fusion.1
  8.7 8.7 all-gather
  18.1 1.4 gather_fusion
  19.5 1.9 fusion.4
  22.7 3.2 convolution_convert_fusion
  27.2 72.4 %all-reduce.18.cloned.1.call-done = bf16[4,512,128]{2,0,1:T(4,128)(2,1)} async-done(((bf16[4,512,128]{2,0,1:T(4,128)(2,1)}), bf16[4,512,128]{2,0,1:T(4,128)(2,1)}) %all-reduce.18.cloned.1.call-update) | async-done | bytes 524304
  101.2 32.1 %all-reduce.16.cloned.1.call-done = bf16[4,64,128]{2,1,0:T(8,128)(2,1)} async-done(((bf16[4,64,128]{2,1,0:T(8,128)(2,1)}), bf16[4,64,128]{2,1,0:T(8,128)(2,1)}) %all-reduce.16.cloned.1.call-update) | async-done | bytes 65552 | tf_op jit(solution)/shard_map/psum | solution.py:28
  134.1 30.7 %all-gather.1 = bf16[1,512,128]{2,1,0:T(8,128)(2,1)S(1)} all-gather(bf16[1,64,128]{2,1,0:T(8,128)(2,1)S(1)} %fusion.76), channel_id=3, replica_groups=mesh['row'=8,'col'=4] {'row'}, dimensions={1}, use_global_device_ids=true | all-gather | bytes 147456 | tf_op jit(solution)/shard_map/all_gather | solution.py:46
  164.9 30.6 %all_gather.29 = bf16[512,128]{1,0:T(8,128)(2,1)S(1)} all-gather(bf16[64,128]{1,0:T(8,128)(2,1)S(1)} %fusion.23), channel_id=1, replica_groups=mesh['row'=8,'col'=4] {'row'}, dimensions={0}, use_global_device_ids=true | all-gather | bytes 147456 | tf_op jit(solution)/shard_map/all_gather | solution.py:50
  195.6 30.5 %all_gather.30 = bf16[512,128]{1,0:T(8,128)(2,1)S(1)} all-gather(bf16[64,128]{1,0:T(8,128)(2,1)S(1)} %fusion.20), channel_id=1, replica_groups=mesh['row'=8,'col'=4] {'row'}, dimensions={0}, use_global_device_ids=true | all-gather | bytes 147456 | tf_op jit(solution)/shard_map/all_gather | solution.py:46
  226.3 30.6 %all_gather.31 = bf16[512,128]{1,0:T(8,128)(2,1)S(1)} all-gather(bf16[64,128]{1,0:T(8,128)(2,1)S(1)} %fusion.24), channel_id=1, replica_groups=mesh['row'=8,'col'=4] {'row'}, dimensions={0}, use_global_device_ids=true | all-gather | bytes 147456 | tf_op jit(solution)/shard_map/all_gather | solution.py:50
  257.1 30.6 %all_gather.32 = bf16[512,128]{1,0:T(8,128)(2,1)S(1)} all-gather(bf16[64,128]{1,0:T(8,128)(2,1)S(1)} %fusion.22), channel_id=1, replica_groups=mesh['row'=8,'col'=4] {'row'}, dimensions={0}, use_global_device_ids=true | all-gather | bytes 147456 | tf_op jit(solution)/shard_map/all_gather | solution.py:46
  287.8 30.6 %all_gather.33 = bf16[512,128]{1,0:T(8,128)(2,1)S(1)} all-gather(bf16[64,128]{1,0:T(8,128)(2,1)S(1)} %fusion.25), channel_id=1, replica_groups=mesh['row'=8,'col'=4] {'row'}, dimensions={0}, use_global_device_ids=true | all-gather | bytes 147456 | tf_op jit(solution)/shard_map/all_gather | solution.py:50
  319.4 30.5 %all_gather.34 = bf16[512,128]{1,0:T(8,128)(2,1)S(1)} all-gather(bf16[64,128]{1,0:T(8,128)(2,1)S(1)} %fusion.21), channel_id=1, replica_groups=mesh['row'=8,'col'=4] {'row'}, dimensions={0}, use_global_device_ids=true | all-gather | bytes 147456 | tf_op jit(solution)/shard_map/all_gather | solution.py:46
  350.1 30.5 %all_gather.35 = bf16[512,128]{1,0:T(8,128)(2,1)S(1)} all-gather(bf16[64,128]{1,0:T(8,128)(2,1)S(1)} %fusion.26), channel_id=1, replica_groups=mesh['row'=8,'col'=4] {'row'}, dimensions={0}, use_global_device_ids=true | all-gather | bytes 147456 | tf_op jit(solution)/shard_map/all_gather | solution.py:50
  381.5 70.7 %all-reduce.8.cloned.1.call-done = bf16[512,128]{0,1:T(8,128)(2,1)} async-done(((bf16[512,128]{0,1:T(8,128)(2,1)}), bf16[512,128]{0,1:T(8,128)(2,1)}) %all-reduce.8.cloned.1.call-update) | async-done | bytes 131088 | tf_op jit(solution)/shard_map/psum | solution.py:73
  454.1 62.9 %reduce-scatter.5.cloned.1.call-done = bf16[64,128]{1,0:T(8,128)(2,1)} async-done(((bf16[512,128]{1,0:T(8,128)(2,1)}), bf16[64,128]{1,0:T(8,128)(2,1)}) %reduce-scatter.5.cloned.1.call-update) | async-done | bytes 16400 | tf_op jit(solution)/shard_map/reduce_scatter | solution.py:64
  516.9 1.6 fusion.14
  519.3 70.9 %all-reduce.10.cloned.1.call-done = bf16[512,128]{0,1:T(8,128)(2,1)} async-done(((bf16[512,128]{0,1:T(8,128)(2,1)}), bf16[512,128]{0,1:T(8,128)(2,1)}) %all-reduce.10.cloned.1.call-update) | async-done | bytes 131088 | tf_op jit(solution)/shard_map/psum | solution.py:73
  591.3 1.8 fusion.10
  593.1 61.9 %reduce-scatter.7.cloned.1.call-done = bf16[64,128]{1,0:T(8,128)(2,1)} async-done(((bf16[512,128]{1,0:T(8,128)(2,1)}), bf16[64,128]{1,0:T(8,128)(2,1)}) %reduce-scatter.7.cloned.1.call-update) | async-done | bytes 16400 | tf_op jit(solution)/shard_map/reduce_scatter | solution.py:64
  655.0 1.6 fusion.15
  656.7 71.8 %all-reduce.12.cloned.1.call-done = bf16[512,128]{0,1:T(8,128)(2,1)} async-done(((bf16[512,128]{0,1:T(8,128)(2,1)}), bf16[512,128]{0,1:T(8,128)(2,1)}) %all-reduce.12.cloned.1.call-update) | async-done | bytes 131088 | tf_op jit(solution)/shard_map/psum | solution.py:73
  729.4 1.8 fusion.11
  731.3 62.1 %reduce-scatter.9.cloned.1.call-done = bf16[64,128]{1,0:T(8,128)(2,1)} async-done(((bf16[512,128]{1,0:T(8,128)(2,1)}), bf16[64,128]{1,0:T(8,128)(2,1)}) %reduce-scatter.9.cloned.1.call-update) | async-done | bytes 16400 | tf_op jit(solution)/shard_map/reduce_scatter | solution.py:64
  793.4 1.6 fusion.16
  795.1 71.8 %all-reduce.14.cloned.1.call-done = bf16[512,128]{0,1:T(8,128)(2,1)} async-done(((bf16[512,128]{0,1:T(8,128)(2,1)}), bf16[512,128]{0,1:T(8,128)(2,1)}) %all-reduce.14.cloned.1.call-update) | async-done | bytes 131088 | tf_op jit(solution)/shard_map/psum | solution.py:73
  868.0 1.4 gather_fusion.1
  869.3 1.5 fusion.7
  870.8 1.3 copy.43
  872.1 2.4 fusion.90
  877.3 19.0 %reduce-scatter.11.cloned.1.call-done = bf16[1,512,128]{2,1,0:T(8,128)(2,1)} async-done(((bf16[4,512,128]{2,1,0:T(8,128)(2,1)}), bf16[1,512,128]{2,1,0:T(8,128)(2,1)}) %reduce-scatter.11.cloned.1.call-update) | async-done | bytes 131088 | tf_op jit(solution)/shard_map/reduce_scatter | solution.py:84
  (94 shorter events, 18.6 us)
Async XLA Ops:
  7.2 12.3 %copy-start = (bf16[1,4,512,512]{3,2,1,0:T(8,128)(2,1)S(1)}, bf16[1,4,512,512]{3,2,1,0:T(8,128)(2,1)}, u32[]{:S(2)}) copy-start(bf16[1,4,512,512]{3,2,1,0:T(8,128)(2,1)} %param.10) | copy-start | bytes 6291460
  7.2 92.4 %all-reduce.18.cloned.1.call-start = ((), (), s32[]{:S(2)}) async-start(), calls=%async_computation.13 | async-start | bytes 1048576
  19.5 3.2 copy-start.14
  21.4 4.6 copy-start.16
  21.4 143.4 %copy-start.2 = (bf16[4,64,512]{2,1,0:T(8,128)(2,1)S(1)}, bf16[4,64,512]{2,1,0:T(8,128)(2,1)}, u32[]{:S(2)}) copy-start(bf16[4,64,512]{2,1,0:T(8,128)(2,1)} %param.14) | copy-start | bytes 786436
  22.7 111.4 %copy-start.13 = (bf16[4,64,128]{2,1,0:T(8,128)(2,1)S(1)}, bf16[4,64,128]{2,1,0:T(8,128)(2,1)}, u32[]{:S(2)}) copy-start(bf16[4,64,128]{2,1,0:T(8,128)(2,1)} %param.13) | copy-start | bytes 196612
  22.7 172.7 %copy-start.3 = (bf16[6,64,512]{2,1,0:T(8,128)(2,1)S(1)}, bf16[6,64,512]{2,1,0:T(8,128)(2,1)}, u32[]{:S(2)}) copy-start(bf16[6,64,512]{2,1,0:T(8,128)(2,1)} %param.15) | copy-start | bytes 1179652
  25.9 107.3 %all-reduce.16.cloned.1.call-start = ((), (), s32[]{:S(2)}) async-start(), calls=%async_computation.12 | async-start | bytes 131072 | tf_op jit(solution)/shard_map/psum | solution.py:28
  101.1 351.1 %all-reduce.8.cloned.1.call-start = ((), (), s32[]{:S(2)}) async-start(), calls=%async_computation.4 | async-start | bytes 262144 | tf_op jit(solution)/shard_map/psum | solution.py:73
  256.9 124.6 %copy-start.12 = (bf16[512,128]{1,0:T(8,128)(2,1)}, bf16[512,128]{1,0:T(8,128)(2,1)S(1)}, u32[]{:S(2)}) copy-start(bf16[512,128]{1,0:T(8,128)(2,1)S(1)} %all_gather.31) | copy-start | bytes 393220
  318.4 411.0 %slice-start = ((bf16[6,64,512]{2,1,0:T(8,128)(2,1)}), bf16[2,64,512]{2,1,0:T(8,128)(2,1)S(1)}, s32[]{:S(2)}) async-start(bf16[6,64,512]{2,1,0:T(8,128)(2,1)} %param.15), calls=%async_computation.14 | async-start | bytes 262144 | tf_op jit(solution)/shard_map/slice | solution.py:57
  319.4 411.9 %copy-start.15 = (s32[1,4]{1,0:T(1,128)S(1)}, s32[1,4]{1,0:T(1,128)}, u32[]{:S(2)}) copy-start(s32[1,4]{1,0:T(1,128)} %param.12) | copy-start | bytes 52
  381.5 135.4 %reduce-scatter.5.cloned.1.call-start = ((), (), s32[]{:S(2)}) async-start(), calls=%async_computation.5 | async-start | bytes 147456 | tf_op jit(solution)/shard_map/reduce_scatter | solution.py:64
  452.2 414.7 %copy-start.10 = (bf16[512,128]{0,1:T(8,128)(2,1)S(1)}, bf16[512,128]{0,1:T(8,128)(2,1)}, u32[]{:S(2)}) copy-start(bf16[512,128]{0,1:T(8,128)(2,1)} %all-reduce.8.cloned.1.call-done) | copy-start | bytes 393220
  453.1 414.8 %copy-start.4 = (bf16[64,128]{0,1:T(8,128)(2,1)}, bf16[64,128]{0,1:T(8,128)(2,1)S(1)}, u32[]{:S(2)}) copy-start(bf16[64,128]{0,1:T(8,128)(2,1)S(1)} %constant_dynamic-slice_fusion.2) | copy-start | bytes 49156
  454.0 136.2 %all-reduce.10.cloned.1.call-start = ((), (), s32[]{:S(2)}) async-start(), calls=%async_computation.6 | async-start | bytes 262144 | tf_op jit(solution)/shard_map/psum | solution.py:73
  518.5 136.5 %reduce-scatter.7.cloned.1.call-start = ((), (), s32[]{:S(2)}) async-start(), calls=%async_computation.7 | async-start | bytes 147456 | tf_op jit(solution)/shard_map/reduce_scatter | solution.py:64
  590.3 276.6 %copy-start.11 = (bf16[512,128]{0,1:T(8,128)(2,1)S(1)}, bf16[512,128]{0,1:T(8,128)(2,1)}, u32[]{:S(2)}) copy-start(bf16[512,128]{0,1:T(8,128)(2,1)} %all-reduce.10.cloned.1.call-done) | copy-start | bytes 393220
  591.2 276.8 %copy-start.6 = (bf16[64,128]{0,1:T(8,128)(2,1)}, bf16[64,128]{0,1:T(8,128)(2,1)S(1)}, u32[]{:S(2)}) copy-start(bf16[64,128]{0,1:T(8,128)(2,1)S(1)} %constant_dynamic-slice_fusion.1) | copy-start | bytes 49156
  593.0 135.4 %all-reduce.12.cloned.1.call-start = ((), (), s32[]{:S(2)}) async-start(), calls=%async_computation.8 | async-start | bytes 262144 | tf_op jit(solution)/shard_map/psum | solution.py:73
  656.6 136.8 %reduce-scatter.9.cloned.1.call-start = ((), (), s32[]{:S(2)}) async-start(), calls=%async_computation.9 | async-start | bytes 147456 | tf_op jit(solution)/shard_map/reduce_scatter | solution.py:64
  729.3 138.6 %copy-start.8 = (bf16[64,128]{0,1:T(8,128)(2,1)}, bf16[64,128]{0,1:T(8,128)(2,1)S(1)}, u32[]{:S(2)}) copy-start(bf16[64,128]{0,1:T(8,128)(2,1)S(1)} %constant_dynamic-slice_fusion) | copy-start | bytes 49156
  731.2 135.7 %all-reduce.14.cloned.1.call-start = ((), (), s32[]{:S(2)}) async-start(), calls=%async_computation.10 | async-start | bytes 262144 | tf_op jit(solution)/shard_map/psum | solution.py:73
  795.0 101.3 %reduce-scatter.11.cloned.1.call-start = ((), (), s32[]{:S(2)}) async-start(), calls=%async_computation.11 | async-start | bytes 655360 | tf_op jit(solution)/shard_map/reduce_scatter | solution.py:84
  872.1 3.3 copy-start.5
  872.1 3.3 copy-start.7
  872.1 3.4 copy-start.9
  872.1 24.2 %copy-start.1 = (bf16[1,512,512]{2,1,0:T(8,128)(2,1)S(1)}, bf16[1,512,512]{2,1,0:T(8,128)(2,1)}, u32[]{:S(2)}) copy-start(bf16[1,512,512]{2,1,0:T(8,128)(2,1)} %param.9) | copy-start | bytes 1572868
Sparse Core Ops, SparseCore 0:
  26.0 73.4 all-reduce.17
  102.5 30.7 all-reduce.15
  381.6 70.5 all-reduce.7
  455.9 60.9 reduce-scatter.4
  520.7 69.5 all-reduce.9
  594.0 60.9 reduce-scatter.6
  658.9 69.5 all-reduce.11
  732.4 60.9 reduce-scatter.8
  797.3 69.5 all-reduce.13
  875.5 20.7 reduce-scatter.10
where the time goes:
time: 906 us; the launch traced here: 905 us
  waiting for transfers between devices  596 us (66%)
  blocking collectives  253 us (28%)
  matrix products  23.5 us (3%)
  between operations  15.1 us (2%)
  local copies, waits for them, and re-layouts  13.2 us (1%)
    psum x4, waiting for transfers between devices, local(): lax.psum(local_part.astype(jnp.bfloat16), 'row').astype(jnp.float32)  285 us
    reduce_scatter x3, waiting for transfers between devices, local(): lax.psum_scatter(partial_term.astype(jnp.bfloat16), 'row', scatter_dimens...  187 us
    all_gather x4, blocking collectives, local(): lax.all_gather(residue.astype(jnp.bfloat16), 'row', axis=0, tiled=True)  122 us
    all_gather x4, blocking collectives, local(): top_forward.append(lax.all_gather(solved_part, 'row', axis=0, tiled=True))  122 us
    unnamed x11, waiting for transfers between devices  72.5 us
    psum x1, waiting for transfers between devices, local(): whole_sum = lax.psum(coupling.astype(jnp.bfloat16), 'col')  32.1 us
    reduce_scatter x1, waiting for transfers between devices, local(): lax.psum_scatter(terms.astype(jnp.bfloat16), 'col', scatter_dimension=0,...  19 us
  transfers between devices with their start and end apart: 10, of which 10 were waited for; matrix products, arithmetic and copies ran while one was open for 0% of the time, Pallas kernels for 0%

commit v1 on v0

--- a/solution.py
+++ b/solution.py
@@ -43,7 +43,10 @@
                 earlier,
                 preferred_element_type=jnp.float32,
             )
-        whole_residue = lax.all_gather(residue.astype(jnp.bfloat16), "row", axis=0, tiled=True)
+        t0 = residue.astype(jnp.bfloat16)
+        whole_residue = jnp.concatenate(
+            lax.all_to_all(jnp.stack(lax.axis_size("row") * [t0]), "row", 0, 0), axis=0
+        )
         solved_part = jnp.dot(
             top_inv[level], whole_residue, preferred_element_type=jnp.float32
         ).astype(jnp.bfloat16)

time: 906 us -> 826 us (0.912)
  blocking collectives: 253 us -> 163 us
    all_gather x4 -> x0, blocking collectives: 122 us -> none  [local(): lax.all_gather(residue.astype(jnp.bfloat16), 'row', axis=0, tiled=True)]
    all_to_all x0 -> x3, blocking collectives: none -> 32.1 us  [local(): lax.all_to_all(jnp.stack(lax.axis_size('row') * [t0]), 'row', 0, 0)]
  transfers between devices with their start and end apart: 10 -> 11, of which waited for: 10 -> 11; matrix products, arithmetic and copies ran while one was open for 0% -> 0% of each run, Pallas kernels for 0% -> 0%
where the time goes in v1:
time: 826 us; the launch traced here: 825 us
  waiting for transfers between devices  600 us (73%)
  blocking collectives  163 us (20%)
  matrix products  24.2 us (3%)
  between operations  15.1 us (2%)
  local copies, waits for them, and re-layouts  14.6 us (2%)
    psum x4, waiting for transfers between devices, local(): lax.psum(local_part.astype(jnp.bfloat16), 'row').astype(jnp.float32)  282 us
    reduce_scatter x3, waiting for transfers between devices, local(): lax.psum_scatter(partial_term.astype(jnp.bfloat16), 'row', scatter_dimens...  187 us
    all_gather x4, blocking collectives, local(): top_forward.append(lax.all_gather(solved_part, 'row', axis=0, tiled=True))  123 us
    unnamed x11, waiting for transfers between devices  72.5 us
    all_to_all x3, blocking collectives, local(): lax.all_to_all(jnp.stack(lax.axis_size('row') * [t0]), 'row', 0, 0)  32.1 us
    psum x1, waiting for transfers between devices, local(): whole_sum = lax.psum(coupling.astype(jnp.bfloat16), 'col')  32.1 us
    reduce_scatter x1, waiting for transfers between devices, local(): lax.psum_scatter(terms.astype(jnp.bfloat16), 'col', scatter_dimension=0,...  19.1 us
  transfers between devices with their start and end apart: 11, of which 11 were waited for; matrix products, arithmetic and copies ran while one was open for 0% of the time, Pallas kernels for 0%

profile of v1, /device:TPU:0, one launch (start us, length us, event | category | flops | bytes accessed | tf_op | source)
XLA Modules:
  0.0 824.9 jit_solution(13348220008663568363)
XLA Ops:
  7.2 1.5 convolution_convert_fusion.1
  8.7 8.7 %all-gather = bf16[2048,128]{1,0:T(8,128)(2,1)S(1)} all-gather(bf16[512,128]{1,0:T(8,128)(2,1)S(1)} %convolution_convert_fusion.1), channel_id=2, replica_groups=mesh['row'=8,'col'=4] {'col'}, dimensions={0}, use_global_device_ids=true | all-gather | bytes 655360 | tf_op jit(solution)/shard_map/all_gather | solution.py:20
  18.1 1.4 gather_fusion
  19.5 1.9 fusion.4
  22.7 3.2 convolution_convert_fusion
  27.2 72.3 %all-reduce.18.cloned.1.call-done = bf16[4,512,128]{2,0,1:T(4,128)(2,1)} async-done(((bf16[4,512,128]{2,0,1:T(4,128)(2,1)}), bf16[4,512,128]{2,0,1:T(4,128)(2,1)}) %all-reduce.18.cloned.1.call-update) | async-done | bytes 524304
  101.1 32.1 %all-reduce.16.cloned.1.call-done = bf16[4,64,128]{2,1,0:T(8,128)(2,1)} async-done(((bf16[4,64,128]{2,1,0:T(8,128)(2,1)}), bf16[4,64,128]{2,1,0:T(8,128)(2,1)}) %all-reduce.16.cloned.1.call-update) | async-done | bytes 65552 | tf_op jit(solution)/shard_map/psum | solution.py:28
  134.1 12.7 %all_to_all.20 = bf16[8,64,128]{2,1,0:T(8,128)(2,1)S(1)} all-to-all(bf16[8,64,128]{2,1,0:T(8,128)(2,1)S(1)} %stack.56), channel_id=1, replica_groups=mesh['row'=8,'col'=4] {'row'}, dimensions={0} | all-to-all | bytes 262144 | tf_op jit(solution)/shard_map/all_to_all | solution.py:48
  146.9 30.6 %all_gather.16 = bf16[512,128]{1,0:T(8,128)(2,1)S(1)} all-gather(bf16[64,128]{1,0:T(8,128)(2,1)S(1)} %fusion.23), channel_id=1, replica_groups=mesh['row'=8,'col'=4] {'row'}, dimensions={0}, use_global_device_ids=true | all-gather | bytes 147456 | tf_op jit(solution)/shard_map/all_gather | solution.py:53
  177.7 9.7 %all_to_all.21 = bf16[8,64,128]{2,1,0:T(8,128)(2,1)S(1)} all-to-all(bf16[8,64,128]{2,1,0:T(8,128)(2,1)S(1)} %stack.58), channel_id=1, replica_groups=mesh['row'=8,'col'=4] {'row'}, dimensions={0} | all-to-all | bytes 262144 | tf_op jit(solution)/shard_map/all_to_all | solution.py:48
  187.6 30.6 %all_gather.17 = bf16[512,128]{1,0:T(8,128)(2,1)S(1)} all-gather(bf16[64,128]{1,0:T(8,128)(2,1)S(1)} %fusion.24), channel_id=1, replica_groups=mesh['row'=8,'col'=4] {'row'}, dimensions={0}, use_global_device_ids=true | all-gather | bytes 147456 | tf_op jit(solution)/shard_map/all_gather | solution.py:53
  219.2 9.7 %all_to_all.22 = bf16[8,64,128]{2,1,0:T(8,128)(2,1)S(1)} all-to-all(bf16[8,64,128]{2,1,0:T(8,128)(2,1)S(1)} %stack.63), channel_id=1, replica_groups=mesh['row'=8,'col'=4] {'row'}, dimensions={0} | all-to-all | bytes 262144 | tf_op jit(solution)/shard_map/all_to_all | solution.py:48
  229.1 30.7 %all_gather.18 = bf16[512,128]{1,0:T(8,128)(2,1)S(1)} all-gather(bf16[64,128]{1,0:T(8,128)(2,1)S(1)} %fusion.25), channel_id=1, replica_groups=mesh['row'=8,'col'=4] {'row'}, dimensions={0}, use_global_device_ids=true | all-gather | bytes 147456 | tf_op jit(solution)/shard_map/all_gather | solution.py:53
  262.0 3.5 all-to-all-start.3
  265.6 7.3 all-to-all-done.3
  273.1 30.6 %all_gather.19 = bf16[512,128]{1,0:T(8,128)(2,1)S(1)} all-gather(bf16[64,128]{1,0:T(8,128)(2,1)S(1)} %fusion.26), channel_id=1, replica_groups=mesh['row'=8,'col'=4] {'row'}, dimensions={0}, use_global_device_ids=true | all-gather | bytes 147456 | tf_op jit(solution)/shard_map/all_gather | solution.py:53
  304.6 67.2 %all-reduce.8.cloned.1.call-done = bf16[512,128]{0,1:T(8,128)(2,1)} async-done(((bf16[512,128]{0,1:T(8,128)(2,1)}), bf16[512,128]{0,1:T(8,128)(2,1)}) %all-reduce.8.cloned.1.call-update) | async-done | bytes 131088 | tf_op jit(solution)/shard_map/psum | solution.py:76
  373.7 62.8 %reduce-scatter.5.cloned.1.call-done = bf16[64,128]{1,0:T(8,128)(2,1)} async-done(((bf16[512,128]{1,0:T(8,128)(2,1)}), bf16[64,128]{1,0:T(8,128)(2,1)}) %reduce-scatter.5.cloned.1.call-update) | async-done | bytes 16400 | tf_op jit(solution)/shard_map/reduce_scatter | solution.py:67
  436.6 1.6 fusion.14
  439.0 70.9 %all-reduce.10.cloned.1.call-done = bf16[512,128]{0,1:T(8,128)(2,1)} async-done(((bf16[512,128]{0,1:T(8,128)(2,1)}), bf16[512,128]{0,1:T(8,128)(2,1)}) %all-reduce.10.cloned.1.call-update) | async-done | bytes 131088 | tf_op jit(solution)/shard_map/psum | solution.py:76
  510.9 1.8 fusion.10
  512.7 61.9 %reduce-scatter.7.cloned.1.call-done = bf16[64,128]{1,0:T(8,128)(2,1)} async-done(((bf16[512,128]{1,0:T(8,128)(2,1)}), bf16[64,128]{1,0:T(8,128)(2,1)}) %reduce-scatter.7.cloned.1.call-update) | async-done | bytes 16400 | tf_op jit(solution)/shard_map/reduce_scatter | solution.py:67
  574.6 1.6 fusion.15
  576.3 71.8 %all-reduce.12.cloned.1.call-done = bf16[512,128]{0,1:T(8,128)(2,1)} async-done(((bf16[512,128]{0,1:T(8,128)(2,1)}), bf16[512,128]{0,1:T(8,128)(2,1)}) %all-reduce.12.cloned.1.call-update) | async-done | bytes 131088 | tf_op jit(solution)/shard_map/psum | solution.py:76
  649.1 1.8 fusion.11
  651.0 62.1 %reduce-scatter.9.cloned.1.call-done = bf16[64,128]{1,0:T(8,128)(2,1)} async-done(((bf16[512,128]{1,0:T(8,128)(2,1)}), bf16[64,128]{1,0:T(8,128)(2,1)}) %reduce-scatter.9.cloned.1.call-update) | async-done | bytes 16400 | tf_op jit(solution)/shard_map/reduce_scatter | solution.py:67
  713.0 1.6 fusion.16
  714.7 71.8 %all-reduce.14.cloned.1.call-done = bf16[512,128]{0,1:T(8,128)(2,1)} async-done(((bf16[512,128]{0,1:T(8,128)(2,1)}), bf16[512,128]{0,1:T(8,128)(2,1)}) %all-reduce.14.cloned.1.call-update) | async-done | bytes 131088 | tf_op jit(solution)/shard_map/psum | solution.py:76
  787.6 1.4 gather_fusion.1
  789.0 1.5 fusion.7
  791.8 2.4 fusion.90
  796.9 19.1 %reduce-scatter.11.cloned.1.call-done = bf16[1,512,128]{2,1,0:T(8,128)(2,1)} async-done(((bf16[4,512,128]{2,1,0:T(8,128)(2,1)}), bf16[1,512,128]{2,1,0:T(8,128)(2,1)}) %reduce-scatter.11.cloned.1.call-update) | async-done | bytes 131088 | tf_op jit(solution)/shard_map/reduce_scatter | solution.py:87
  (101 shorter events, 22.0 us)
Async XLA Ops:
  7.2 12.3 %copy-start = (bf16[1,4,512,512]{3,2,1,0:T(8,128)(2,1)S(1)}, bf16[1,4,512,512]{3,2,1,0:T(8,128)(2,1)}, u32[]{:S(2)}) copy-start(bf16[1,4,512,512]{3,2,1,0:T(8,128)(2,1)} %param.10) | copy-start | bytes 6291460
  7.2 92.4 %all-reduce.18.cloned.1.call-start = ((), (), s32[]{:S(2)}) async-start(), calls=%async_computation.17 | async-start | bytes 1048576
  19.5 3.3 copy-start.15
  21.4 4.6 copy-start.17
  21.4 125.4 %copy-start.2 = (bf16[4,64,512]{2,1,0:T(8,128)(2,1)S(1)}, bf16[4,64,512]{2,1,0:T(8,128)(2,1)}, u32[]{:S(2)}) copy-start(bf16[4,64,512]{2,1,0:T(8,128)(2,1)} %param.14) | copy-start | bytes 786436
  22.7 111.3 %copy-start.14 = (bf16[4,64,128]{2,1,0:T(8,128)(2,1)S(1)}, bf16[4,64,128]{2,1,0:T(8,128)(2,1)}, u32[]{:S(2)}) copy-start(bf16[4,64,128]{2,1,0:T(8,128)(2,1)} %param.13) | copy-start | bytes 196612
  22.7 154.8 %copy-start.3 = (bf16[6,64,512]{2,1,0:T(8,128)(2,1)S(1)}, bf16[6,64,512]{2,1,0:T(8,128)(2,1)}, u32[]{:S(2)}) copy-start(bf16[6,64,512]{2,1,0:T(8,128)(2,1)} %param.15) | copy-start | bytes 1179652
  25.9 107.3 %all-reduce.16.cloned.1.call-start = ((), (), s32[]{:S(2)}) async-start(), calls=%async_computation.16 | async-start | bytes 131072 | tf_op jit(solution)/shard_map/psum | solution.py:28
  218.3 155.4 %copy-start.12 = (bf16[512,128]{1,0:T(8,128)(2,1)}, bf16[512,128]{1,0:T(8,128)(2,1)S(1)}, u32[]{:S(2)}) copy-start(bf16[512,128]{1,0:T(8,128)(2,1)S(1)} %all_gather.17) | copy-start | bytes 393220
  259.8 0.7 copy-start.13
  261.4 387.7 %slice-start = ((bf16[6,64,512]{2,1,0:T(8,128)(2,1)}), bf16[2,64,512]{2,1,0:T(8,128)(2,1)S(1)}, s32[]{:S(2)}) async-start(bf16[6,64,512]{2,1,0:T(8,128)(2,1)} %param.15), calls=%async_computation.18 | async-start | bytes 262144 | tf_op jit(solution)/shard_map/slice | solution.py:60
  262.0 388.9 %copy-start.16 = (s32[1,4]{1,0:T(1,128)S(1)}, s32[1,4]{1,0:T(1,128)}, u32[]{:S(2)}) copy-start(s32[1,4]{1,0:T(1,128)} %param.12) | copy-start | bytes 52
  262.0 10.9 %all-to-all-start.3 = ((bf16[8,64,128]{2,1,0:T(8,128)(2,1)}), bf16[8,64,128]{2,1,0:T(8,128)(2,1)S(1)}, u32[]{:S(2)}, u32[]{:S(2)}) async-start(bf16[8,64,128]{2,1,0:T(8,128)(2,1)} %stack.130), calls=%async_computation.3 | async-start | bytes 262144 | tf_op jit(solution)/shard_map/all_to_all | solution.py:48
  265.6 106.3 %all-reduce.8.cloned.1.call-start = ((), (), s32[]{:S(2)}) async-start(), calls=%async_computation.8 | async-start | bytes 262144 | tf_op jit(solution)/shard_map/psum | solution.py:76
  304.6 132.0 %reduce-scatter.5.cloned.1.call-start = ((), (), s32[]{:S(2)}) async-start(), calls=%async_computation.9 | async-start | bytes 147456 | tf_op jit(solution)/shard_map/reduce_scatter | solution.py:67
  371.8 414.7 %copy-start.10 = (bf16[512,128]{0,1:T(8,128)(2,1)S(1)}, bf16[512,128]{0,1:T(8,128)(2,1)}, u32[]{:S(2)}) copy-start(bf16[512,128]{0,1:T(8,128)(2,1)} %all-reduce.8.cloned.1.call-done) | copy-start | bytes 393220
  372.7 414.8 %copy-start.4 = (bf16[64,128]{0,1:T(8,128)(2,1)}, bf16[64,128]{0,1:T(8,128)(2,1)S(1)}, u32[]{:S(2)}) copy-start(bf16[64,128]{0,1:T(8,128)(2,1)S(1)} %constant_dynamic-slice_fusion.2) | copy-start | bytes 49156
  373.7 136.2 %all-reduce.10.cloned.1.call-start = ((), (), s32[]{:S(2)}) async-start(), calls=%async_computation.10 | async-start | bytes 262144 | tf_op jit(solution)/shard_map/psum | solution.py:76
  438.2 136.4 %reduce-scatter.7.cloned.1.call-start = ((), (), s32[]{:S(2)}) async-start(), calls=%async_computation.11 | async-start | bytes 147456 | tf_op jit(solution)/shard_map/reduce_scatter | solution.py:67
  509.9 276.6 %copy-start.11 = (bf16[512,128]{0,1:T(8,128)(2,1)S(1)}, bf16[512,128]{0,1:T(8,128)(2,1)}, u32[]{:S(2)}) copy-start(bf16[512,128]{0,1:T(8,128)(2,1)} %all-reduce.10.cloned.1.call-done) | copy-start | bytes 393220
  510.8 276.8 %copy-start.6 = (bf16[64,128]{0,1:T(8,128)(2,1)}, bf16[64,128]{0,1:T(8,128)(2,1)S(1)}, u32[]{:S(2)}) copy-start(bf16[64,128]{0,1:T(8,128)(2,1)S(1)} %constant_dynamic-slice_fusion.1) | copy-start | bytes 49156
  512.7 135.4 %all-reduce.12.cloned.1.call-start = ((), (), s32[]{:S(2)}) async-start(), calls=%async_computation.12 | async-start | bytes 262144 | tf_op jit(solution)/shard_map/psum | solution.py:76
  576.3 136.8 %reduce-scatter.9.cloned.1.call-start = ((), (), s32[]{:S(2)}) async-start(), calls=%async_computation.13 | async-start | bytes 147456 | tf_op jit(solution)/shard_map/reduce_scatter | solution.py:67
  649.0 138.6 %copy-start.8 = (bf16[64,128]{0,1:T(8,128)(2,1)}, bf16[64,128]{0,1:T(8,128)(2,1)S(1)}, u32[]{:S(2)}) copy-start(bf16[64,128]{0,1:T(8,128)(2,1)S(1)} %constant_dynamic-slice_fusion) | copy-start | bytes 49156
  650.9 135.7 %all-reduce.14.cloned.1.call-start = ((), (), s32[]{:S(2)}) async-start(), calls=%async_computation.14 | async-start | bytes 262144 | tf_op jit(solution)/shard_map/psum | solution.py:76
  714.6 101.4 %reduce-scatter.11.cloned.1.call-start = ((), (), s32[]{:S(2)}) async-start(), calls=%async_computation.15 | async-start | bytes 655360 | tf_op jit(solution)/shard_map/reduce_scatter | solution.py:87
  791.8 3.3 copy-start.5
  791.8 3.4 copy-start.7
  791.8 3.5 copy-start.9
  791.8 24.2 %copy-start.1 = (bf16[1,512,512]{2,1,0:T(8,128)(2,1)S(1)}, bf16[1,512,512]{2,1,0:T(8,128)(2,1)}, u32[]{:S(2)}) copy-start(bf16[1,512,512]{2,1,0:T(8,128)(2,1)} %param.9) | copy-start | bytes 1572868
Sparse Core Ops, SparseCore 0:
  26.1 73.4 all-reduce.17
  102.4 30.7 all-reduce.15
  304.7 67.1 all-reduce.7
  375.6 60.9 reduce-scatter.4
  440.3 69.5 all-reduce.9
  513.6 60.9 reduce-scatter.6
  578.6 69.5 all-reduce.11
  652.0 60.9 reduce-scatter.8
  717.0 69.5 all-reduce.13
  795.2 20.7 reduce-scatter.10
